TPU v7x, 32 devices: a whole 2x2x4 slice. The times are simulated.
32 devices in a mesh: rep: 4 (over z), sy: 2 (over y), sx: 4 (over x, core).
Axes of the slice: x: 2, y: 2, z: 4, core: 2. Of those that a mesh axis runs over, the one named last changes fastest.
Arguments:
- features: bfloat16 [4, 32, 64, 256], P('rep', 'sy', 'sx'), may hold values from -1.5 to 1.5
- cotangent: bfloat16 [4, 32, 64, 256], P('rep', 'sy', 'sx'), may hold values from -15 to 15
- gain_conv: float32 [256], replicated, may hold values from 0.25 to 1.75
- expand_weight: bfloat16 [256, 1024], replicated, may hold values from -0.375 to 0.375
- dw_kernel: float32 [1024, 9], replicated, may hold values from -2 to 2
- project_weight: bfloat16 [1024, 256], replicated, may hold values from -0.1875 to 0.1875
- gain_block: float32 [256], replicated, may hold values from 0.25 to 1.75
- block_inward: bfloat16 [256, 768], replicated, may hold values from -0.375 to 0.375
- block_outward: bfloat16 [256, 256], replicated, may hold values from -0.375 to 0.375
- gain_grid: float32 [256], replicated, may hold values from 0.25 to 1.75
- grid_inward: bfloat16 [256, 768], replicated, may hold values from -0.375 to 0.375
- grid_outward: bfloat16 [256, 256], replicated, may hold values from -0.375 to 0.375
Outputs:
- output_tokens: bfloat16 [4, 32, 64, 256], P('rep', 'sy', 'sx')
- token_grads: bfloat16 [4, 32, 64, 256], P('rep', 'sy', 'sx')
- grad_conv_gain: float32 [256], P('rep')
- grad_expand: float32 [256, 1024], P('rep')
- grad_kernel: float32 [1024, 9], P('rep')
- grad_project: float32 [1024, 256], P('rep')
- grad_block_gain: float32 [256], P('rep')
- grad_block_inward: float32 [256, 768], P('rep')
- grad_block_outward: float32 [256, 256], P('rep')
- grad_grid_gain: float32 [256], P('rep')
- grad_grid_inward: float32 [256, 768], P('rep')
- grad_grid_outward: float32 [256, 256], P('rep')
All inputs are finite; a program needn't handle non-finite values.
Results may differ from a plain program's by a relative error of at most 0.018.
Values may be sent and summed in bfloat16 or wider, within the bound.
No kernel may reach another device: no remote copies, remote signals or barrier semaphores. Data moves between devices by JAX's collectives and lax.ppermute only.
A program may use at most 64 MiB of HBM per device.

v0:
```python
import jax
import jax.numpy as jnp
from jax import lax
from jax.sharding import PartitionSpec as P

HEADS = 8
WIN = 8
EPSILON = 1e-05


def as_sent(value):

    def short(part):
        return part.astype(jnp.bfloat16) if part.dtype == jnp.float32 else part

    return jax.tree.map(short, value)


def extended_2(cells, sides, width):
    for axis, dim in sides:
        count = lax.axis_size(axis)
        ends = count - 1
        head = lax.slice_in_dim(cells, 0, width, axis=dim)
        tail = lax.slice_in_dim(cells, cells.shape[dim] - width, cells.shape[dim], axis=dim)
        cells = jnp.concatenate(
            [
                lax.ppermute(tail, axis, [(i, (i + 1) % count) for i in range(ends)]),
                cells,
                lax.ppermute(head, axis, [((i + 1) % count, i) for i in range(ends)]),
            ],
            axis=dim,
        )
    return cells


def widen(values):
    return lax.optimization_barrier(values).astype(jnp.float32)


def layer_norm(values, gain):
    row_mean = jnp.mean(values, axis=-1, keepdims=True)
    centred = values - row_mean
    variance = jnp.mean(centred * centred, axis=-1, keepdims=True)
    return centred * lax.rsqrt(variance + EPSILON) * gain


def project_rows(values, weight):
    leading = values.shape[:-1]
    flattened = values.reshape(-1, values.shape[-1])
    product = jnp.dot(flattened, weight, preferred_element_type=jnp.float32)
    return product.reshape(leading + (weight.shape[1],))


def outer_sum(left_side, right_side):
    left_flat = left_side.reshape(-1, left_side.shape[-1])
    right_flat = right_side.reshape(-1, right_side.shape[-1]).astype(jnp.bfloat16)
    return lax.dot_general(
        left_flat, right_flat, (((0,), (0,)), ((), ())), preferred_element_type=jnp.float32
    )


def to_windows(image, side):
    height, breadth, channels = image.shape
    blocks = image.reshape(height // side, side, breadth // side, side, channels)
    return blocks.transpose(0, 2, 1, 3, 4).reshape(-1, side * side, channels)


def from_windows(windows, height, breadth, side):
    channels = windows.shape[-1]
    blocks = windows.reshape(height // side, breadth // side, side, side, channels)
    return blocks.transpose(0, 2, 1, 3, 4).reshape(height, breadth, channels)


def to_grid(image, side):
    height, breadth, channels = image.shape
    blocks = image.reshape(side, height // side, side, breadth // side, channels)
    return blocks.transpose(1, 3, 0, 2, 4).reshape(-1, side * side, channels)


def from_grid(windows, height, breadth, side):
    channels = windows.shape[-1]
    blocks = windows.reshape(height // side, breadth // side, side, side, channels)
    return blocks.transpose(2, 0, 3, 1, 4).reshape(height, breadth, channels)


def window_attention(windows, weight, tap_in, heads):
    count, members, channels = windows.shape
    head_width = channels // heads
    qkv_rows = (project_rows(windows, weight) + tap_in).astype(jnp.bfloat16)
    queries = qkv_rows[..., :channels].reshape(count, members, heads, head_width)
    key_rows = qkv_rows[..., channels : 2 * channels].reshape(count, members, heads, head_width)
    value_rows = qkv_rows[..., 2 * channels :].reshape(count, members, heads, head_width)
    scores = jnp.einsum(
        "wqhd,wkhd->whqk", queries, key_rows, preferred_element_type=jnp.float32
    ) * head_width ** (-0.5)
    softmax_out = jax.nn.softmax(scores, axis=-1).astype(jnp.bfloat16)
    attended = jnp.einsum(
        "whqk,wkhd->wqhd", softmax_out, value_rows, preferred_element_type=jnp.float32
    )
    return attended.astype(jnp.bfloat16).reshape(count, members, channels)


def depthwise(extended, kernel):
    height = extended.shape[0] - 2
    breadth = extended.shape[1] - 2
    widened = widen(extended)
    summed = jnp.zeros((height, breadth, extended.shape[2]), jnp.float32)
    for tap_index in range(9):
        row_step, col_step = divmod(tap_index, 3)
        summed = (
            summed
            + widened[row_step : row_step + height, col_step : col_step + breadth]
            * kernel[:, tap_index]
        )
    return summed


def depthwise_back(grad_ext, kernel):
    height = grad_ext.shape[0] - 2
    breadth = grad_ext.shape[1] - 2
    summed = jnp.zeros((height, breadth, grad_ext.shape[2]), jnp.float32)
    for tap_index in range(9):
        row_step, col_step = divmod(tap_index, 3)
        summed = (
            summed
            + grad_ext[2 - row_step : 2 - row_step + height, 2 - col_step : 2 - col_step + breadth]
            * kernel[:, tap_index]
        )
    return summed


def swap_blocks(blocks):
    sy_count, sx_count, row_part, col_part, channels = blocks.shape
    flattened = blocks.reshape(sy_count * sx_count, row_part, col_part, channels)
    moved = lax.all_to_all(
        as_sent(flattened), ("sy", "sx"), split_axis=0, concat_axis=0, tiled=True
    ).astype(flattened.dtype)
    return moved.reshape(blocks.shape)


def to_exchanged(image):
    height, breadth, channels = image.shape
    sy_count = lax.axis_size("sy")
    sx_count = lax.axis_size("sx")
    blocks = image.reshape(height // sy_count, sy_count, breadth // sx_count, sx_count, channels)
    moved = swap_blocks(blocks.transpose(1, 3, 0, 2, 4))
    return moved.transpose(0, 2, 1, 3, 4).reshape(height, breadth, channels)


def to_home(image):
    height, breadth, channels = image.shape
    sy_count = lax.axis_size("sy")
    sx_count = lax.axis_size("sx")
    blocks = image.reshape(sy_count, height // sy_count, sx_count, breadth // sx_count, channels)
    moved = swap_blocks(blocks.transpose(0, 2, 1, 3, 4))
    return moved.transpose(2, 0, 3, 1, 4).reshape(height, breadth, channels)


def body(
    features,
    cotangent,
    gain_conv,
    expand_weight,
    dw_kernel,
    project_weight,
    gain_block,
    block_inward,
    block_outward,
    gain_grid,
    grid_inward,
    grid_outward,
):
    image = features[0]
    height, breadth, channels = image.shape
    expand_units = expand_weight.shape[1]
    window_count = height * breadth // (WIN * WIN)
    zero_width = jnp.zeros((height, breadth, channels), jnp.float32)
    zero_expand = jnp.zeros((height, breadth, expand_units), jnp.float32)
    zero_qkv = jnp.zeros((window_count, WIN * WIN, 3 * channels), jnp.float32)
    widened = image.astype(jnp.float32)

    def conv_front(wide_in, gain_in):
        return layer_norm(wide_in, gain_in).astype(jnp.bfloat16)

    normed, front_back = jax.vjp(conv_front, widened, gain_conv)

    def expand_fn(normed_in, tap_in):
        return jax.nn.gelu(project_rows(normed_in, expand_weight) + tap_in).astype(jnp.bfloat16)

    inner, expand_back = jax.vjp(expand_fn, normed, zero_expand)
    inner_ext = extended_2(inner, (("sy", 0), ("sx", 1)), 1)

    def conv_only(kernel_in):
        return depthwise(inner_ext, kernel_in)

    conv_out, kernel_back = jax.vjp(conv_only, dw_kernel)

    def conv_tail(conv_in, wide_in, tap_in):
        activated_in = jax.nn.gelu(conv_in).astype(jnp.bfloat16)
        return (wide_in + project_rows(activated_in, project_weight) + tap_in, activated_in)

    stream_one, tail_back, activated = jax.vjp(
        conv_tail, conv_out, widened, zero_width, has_aux=True
    )

    def block_layer(stream_in, gain_in, tap_in, tap_out):
        normed_two = layer_norm(stream_in, gain_in).astype(jnp.bfloat16)
        windows = to_windows(normed_two, WIN)
        attended = window_attention(windows, block_inward, tap_in, HEADS)
        attended_home = from_windows(attended, height, breadth, WIN)
        return (
            stream_in + project_rows(attended_home, block_outward) + tap_out,
            (windows, attended_home),
        )

    stream_two, block_back, block_saved = jax.vjp(
        block_layer, stream_one, gain_block, zero_qkv, zero_width, has_aux=True
    )

    def grid_front(stream_in, gain_in):
        return layer_norm(stream_in, gain_in).astype(jnp.bfloat16)

    normed_three, grid_front_back = jax.vjp(grid_front, stream_two, gain_grid)
    grid_windows = to_grid(to_exchanged(normed_three), WIN)

    def grid_core(windows_in, tap_in):
        return window_attention(windows_in, grid_inward, tap_in, HEADS)

    grid_attended, grid_core_back = jax.vjp(grid_core, grid_windows, zero_qkv)
    grid_home = to_home(from_grid(grid_attended, height, breadth, WIN))

    def grid_tail(stream_in, attended_in, tap_in):
        return (stream_in + project_rows(attended_in, grid_outward) + tap_in).astype(jnp.bfloat16)

    output_tile, grid_tail_back = jax.vjp(grid_tail, stream_two, grid_home, zero_width)
    d_stream_two, d_grid_home, tap_grid_out = grid_tail_back(cotangent[0])
    d_grid_attended = to_grid(to_exchanged(d_grid_home), WIN)
    d_grid_windows, tap_grid_in = grid_core_back(d_grid_attended)
    d_normed_three = to_home(from_grid(d_grid_windows, height, breadth, WIN))
    d_stream_extra, d_gain_grid = grid_front_back(d_normed_three)
    d_stream_two = d_stream_two + d_stream_extra
    d_stream_one, d_gain_block, tap_block_in, tap_block_out = block_back(d_stream_two)
    d_conv, d_wide_tail, tap_project = tail_back(d_stream_one)
    d_conv_ext = extended_2(d_conv, (("sy", 0), ("sx", 1)), 1)
    d_kernel = kernel_back(d_conv)[0]
    d_inner = depthwise_back(d_conv_ext, dw_kernel).astype(jnp.bfloat16)
    d_normed, tap_expand = expand_back(d_inner)
    d_wide_front, d_gain_conv = front_back(d_normed)
    token_grad = (d_wide_tail + d_wide_front).astype(jnp.bfloat16)
    local_grads = (
        d_gain_conv,
        outer_sum(normed, tap_expand),
        d_kernel,
        outer_sum(activated, tap_project),
        d_gain_block,
        outer_sum(block_saved[0], tap_block_in),
        outer_sum(block_saved[1], tap_block_out),
        d_gain_grid,
        outer_sum(grid_windows, tap_grid_in),
        outer_sum(grid_home, tap_grid_out),
    )
    whole_sums = lax.psum(
        (
            local_grads[0],
            local_grads[1],
            local_grads[2],
            local_grads[3],
            local_grads[4],
            local_grads[5],
            local_grads[6],
            local_grads[7],
            local_grads[8],
            local_grads[9],
        ),
        ("sy", "sx"),
    )
    summed = (
        lax.psum_scatter(whole_sums[0], "rep", scatter_dimension=0, tiled=True),
        lax.psum_scatter(whole_sums[1], "rep", scatter_dimension=0, tiled=True),
        lax.psum_scatter(whole_sums[2], "rep", scatter_dimension=0, tiled=True),
        lax.psum_scatter(whole_sums[3], "rep", scatter_dimension=0, tiled=True),
        lax.psum_scatter(whole_sums[4], "rep", scatter_dimension=0, tiled=True),
        lax.psum_scatter(whole_sums[5], "rep", scatter_dimension=0, tiled=True),
        lax.psum_scatter(whole_sums[6], "rep", scatter_dimension=0, tiled=True),
        lax.psum_scatter(whole_sums[7], "rep", scatter_dimension=0, tiled=True),
        lax.psum_scatter(whole_sums[8], "rep", scatter_dimension=0, tiled=True),
        lax.psum_scatter(whole_sums[9], "rep", scatter_dimension=0, tiled=True),
    )
    return (
        output_tile[None],
        token_grad[None],
        summed[0],
        summed[1],
        summed[2],
        summed[3],
        summed[4],
        summed[5],
        summed[6],
        summed[7],
        summed[8],
        summed[9],
    )


def solution(mesh):
    return jax.shard_map(
        body,
        mesh=mesh,
        in_specs=(
            P("rep", "sy", "sx", None),
            P("rep", "sy", "sx", None),
            P(),
            P(),
            P(),
            P(),
            P(),
            P(),
            P(),
            P(),
            P(),
            P(),
        ),
        out_specs=(
            P("rep", "sy", "sx", None),
            P("rep", "sy", "sx", None),
            P("rep"),
            P("rep", None),
            P("rep", None),
            P("rep", None),
            P("rep"),
            P("rep", None),
            P("rep", None),
            P("rep"),
            P("rep", None),
            P("rep", None),
        ),
        check_vma=False,
    )
```

profile of v0, /device:TPU:0, one launch (start us, length us, event | category | flops | bytes accessed | tf_op | source)
XLA Modules:
  0.0 337.4 jit_solution(8117348626632107201)
XLA Ops:
  9.5 2.4 multiply_convert_fusion.1
  11.8 1.4 collective-permute-start.1
  13.3 4.9 %collective-permute-start = (bf16[1,16,1024]{2,1,0:T(8,128)(2,1)S(1)}, bf16[1,16,1024]{2,1,0:T(8,128)(2,1)S(1)}, u32[]{:S(2)}, u32[]{:S(2)}) collective-permute-start(bf16[1,16,1024]{2,1,0:T(8,128)(2,1)S(1)} %get-tuple-element.51), channel_id=1, source_target_pairs={{0,4},{1,5},{2,6},{3,7},{8,12},{9,13},{10,14},{11,15},{16,20},{17,... | collective-permute-start | bytes 98312 | tf_op jit(solution)/shard_map/ppermute | solution.py:27
  19.2 4.0 %all-to-all-start.2 = ((bf16[8,8,4,256]{3,1,2,0:T(8,128)(2,1)}), bf16[8,8,4,256]{3,1,2,0:T(8,128)(2,1)}, u32[]{:S(2)}, u32[]{:S(2)}) async-start(bf16[8,8,4,256]{3,1,2,0:T(8,128)(2,1)} %bitcast.44), calls=%async_computation.2 | async-start | bytes 262144 | tf_op jit(solution)/shard_map/all_to_all | solution.py:135
  23.3 1.3 collective-permute-start.3
  24.6 3.0 collective-permute-start.2
  33.3 3.2 fusion.105
  36.5 1.5 fusion.6
  39.3 1.2 fusion.106
  42.3 6.7 %all-to-all-start = ((bf16[8,8,4,256]{3,1,2,0:T(8,128)(2,1)}), bf16[8,8,4,256]{3,1,2,0:T(8,128)(2,1)}, u32[]{:S(2)}, u32[]{:S(2)}) async-start(bf16[8,8,4,256]{3,1,2,0:T(8,128)(2,1)} %bitcast.24), calls=%async_computation | async-start | bytes 262144 | tf_op jit(solution)/shard_map/all_to_all | solution.py:135
  50.8 1.2 reshape_reshape.26
  53.1 1.6 all-to-all-done
  55.8 1.3 convolution_convert_fusion.3
  57.8 1.7 copy.143
  59.5 1.7 copy.144
  62.1 2.6 fusion.107
  64.7 1.8 fusion.15
  69.8 1.8 copy.160
  71.6 1.7 copy.158
  73.3 1.7 copy.156
  77.4 7.9 %all_to_all.20 = bf16[8,8,4,256]{3,1,2,0:T(8,128)(2,1)S(1)} all-to-all(bf16[8,8,4,256]{3,1,2,0:T(8,128)(2,1)S(1)} %bitcast.291), channel_id=1, replica_groups=mesh['rep'=4,'sy'=2,'sx'=4] {'sy','sx'}, dimensions={0} | all-to-all | bytes 262144 | tf_op jit(solution)/shard_map/all_to_all | solution.py:135
  88.2 1.5 multiply_reduce_fusion.9
  89.7 1.6 fusion.96
  92.5 2.2 fusion.7
  94.7 2.1 copy.147
  96.8 2.1 reshape.413
  98.9 1.7 copy.148
  100.6 1.6 reshape_reshape.24
  103.1 7.9 %all_to_all.21 = bf16[8,8,4,256]{3,1,2,0:T(8,128)(2,1)S(1)} all-to-all(bf16[8,8,4,256]{3,1,2,0:T(8,128)(2,1)S(1)} %bitcast.293), channel_id=1, replica_groups=mesh['rep'=4,'sy'=2,'sx'=4] {'sy','sx'}, dimensions={0} | all-to-all | bytes 262144 | tf_op jit(solution)/shard_map/all_to_all | solution.py:135
  111.8 1.6 reshape_reshape.29
  113.4 1.9 fusion.112
  115.3 1.3 multiply_divide_fusion
  116.7 1.2 fusion.111
  117.9 1.2 fusion.114
  119.8 1.2 reshape.428
  122.1 1.9 fusion.20
  124.0 1.9 convolution_convert_fusion.5
  127.0 2.5 convolution_convert_fusion.6
  129.5 1.7 copy.170
  131.2 2.4 convolution_convert_fusion.7
  133.7 1.7 copy.167
  136.8 2.1 fusion.109
  139.9 1.1 add_add_fusion.4
  142.3 1.6 convolution_bitcast_fusion
  144.1 3.7 %multiply_reduce_fusion.8 = (f32[1024]{0:T(1024)S(1)}, f32[1024]{0:T(1024)S(1)}, f32[1024]{0:T(1024)S(1)}, f32[1024]{0:T(1024)S(1)}, f32[1024]{0:T(1024)S(1)}, /...) fusion(f32[18,18,1024]{2,1,0:T(8,128)S(1)} %convert_element_typ, ...), kind=kLoop, calls=%fused_computation.104 | loop fusion | flops 14408704 | bytes 11083776 | tf_op jit(solution)/shard_map/transpose(jvp())/reduce_sum | solution.py:112
  147.8 1.3 collective-permute-start.5
  149.1 4.5 %collective-permute-start.4 = (f32[1,16,1024]{2,1,0:T(8,128)S(1)}, f32[1,16,1024]{2,1,0:T(8,128)S(1)}, u32[]{:S(2)}, u32[]{:S(2)}) collective-permute-start(f32[1,16,1024]{2,1,0:T(8,128)S(1)} %get-tuple-element.47), channel_id=1, source_target_pairs={{0,4},{1,5},{2,6},{3,7},{8,12},{9,13},{10,14},{11,15},{16,20},{17,... | collective-permute-start | bytes 196616 | tf_op jit(solution)/shard_map/ppermute | solution.py:27
  153.9 1.6 collective-permute-done.4
  155.6 1.3 collective-permute-start.6
  156.9 3.0 collective-permute-start.7
  161.4 1.9 fusion.22
  163.3 1.3 fusion.108
  168.5 15.5 %reduce-scatter.14.cloned.1.call-done = f32[64,768]{1,0:T(8,128)} async-done(((f32[256,768]{1,0:T(8,128)}), f32[64,768]{1,0:T(8,128)}) %reduce-scatter.14.cloned.1.call-update) | async-done | bytes 196624 | tf_op jit(solution)/shard_map/reduce_scatter | solution.py:283
  184.1 28.8 %reduce-scatter.12.cloned.1.call-done = f32[256,256]{1,0:T(8,128)} async-done(((f32[1024,256]{1,0:T(8,128)}), f32[256,256]{1,0:T(8,128)}) %reduce-scatter.12.cloned.1.call-update) | async-done | bytes 262160 | tf_op jit(solution)/shard_map/reduce_scatter | solution.py:281
  212.8 28.1 %reduce-scatter.8.cloned.1.call-done = f32[64,1024]{1,0:T(8,128)} async-done(((f32[256,1024]{1,0:T(8,128)}), f32[64,1024]{1,0:T(8,128)}) %reduce-scatter.8.cloned.1.call-update) | async-done | bytes 262160 | tf_op jit(solution)/shard_map/reduce_scatter | solution.py:279
  241.3 9.4 %all-reduce.20 = (f32[256]{0:T(256)S(1)}, f32[256]{0:T(256)S(1)}, f32[256]{0:T(256)S(1)}) all-reduce(f32[256]{0:T(256)S(1)} %get-tuple-element.25, f32[256]{0:T(256)S(1)} %copy-done.52, f32[256]{0:T(256)S(1)} %copy-done.51), channel_id=2, replica_groups=mesh['rep'=4,'sy'=2,'sx'=4] {'rep'}, use_global_device_ids=true, to_apply=%region_20.0.clone | all-reduce | flops 768 | bytes 6144
  250.9 10.5 %reduce-scatter.10.cloned.1.call-done = f32[256,9]{0,1:T(8,128)} async-done(((f32[1024,9]{0,1:T(8,128)}), f32[256,9]{0,1:T(8,128)}) %reduce-scatter.10.cloned.1.call-update) | async-done | bytes 9232 | tf_op jit(solution)/shard_map/reduce_scatter | solution.py:280
  261.5 23.7 %all-reduce.18 = (f32[64]{0:T(128)}, f32[256,9]{0,1:T(8,128)}, f32[64]{0:T(128)}, f32[64]{0:T(128)}) all-reduce(f32[64]{0:T(128)S(1)} %dynamic-slice.1, f32[256,9]{0,1:T(8,128)} %reduce-scatter.10.cloned.1.call-done, f32[64]{0:T(128)S(1)} %dynamic-slice.3, f32[64]{0:T(128)S(1)} %dynamic-slice.5), channel_id=1, replica_groups=mesh['rep'=4,'sy'=2,'sx'=4] {'sy','sx'}, use_global_device_ids=true, to_apply=%region_19.0 | all-reduce | flops 2496 | bytes 19968 | tf_op jit(solution)/shard_map/psum | solution.py:262
  286.0 35.9 %all-reduce.23.cloned.1.call-done = (f32[64,1024]{1,0:T(8,128)}, f32[256,256]{1,0:T(8,128)}, f32[64,768]{1,0:T(8,128)}, f32[64,256]{1,0:T(8,128)}, f32[64,768]{1,0:T(8,128)}, /*index=5*/f32[64,256]{1,0:T(8,128)}) async-done(((f32[64,1024]{1,0:T(8,128)}, f32[256,256]{1,0:T(8,128)}, f32[64,768]{1,0:T(8,128)}, f32[64,256]{1,0:T(8,128)}, f32[64,768]{1,0:T(8,128)}, /*index=5*/f32[64,256]{1,0:T(8,128)}), ...) | async-done | bytes 1048592 | tf_op jit(solution)/shard_map/psum | solution.py:262
  321.9 1.7 copy.199
  323.6 1.7 copy.200
  325.2 1.6 copy.201
  326.9 1.5 copy.202
  328.3 1.6 copy.203
  (231 shorter events, 42.0 us)
Async XLA Ops:
  7.2 2.3 copy-start
  8.3 9.9 %copy-start.8 = (bf16[1,16,16,256]{3,2,1,0:T(8,128)(2,1)S(1)}, bf16[1,16,16,256]{3,2,1,0:T(8,128)(2,1)}, u32[]{:S(2)}) copy-start(bf16[1,16,16,256]{3,2,1,0:T(8,128)(2,1)} %param.13) | copy-start | bytes 393220
  8.3 9.9 %copy-start.20 = (bf16[256,256]{1,0:T(8,128)(2,1)S(1)}, bf16[256,256]{1,0:T(8,128)(2,1)}, u32[]{:S(2)}) copy-start(bf16[256,256]{1,0:T(8,128)(2,1)} %param.23) | copy-start | bytes 393220
  11.8 15.8 %copy-start.45 = (f32[1024,9]{0,1:T(8,128)S(1)}, f32[1024,9]{0,1:T(8,128)}, u32[]{:S(2)}) copy-start(f32[1024,9]{0,1:T(8,128)} %param.16) | copy-start | bytes 110596
  11.8 11.3 %collective-permute-start.1 = (bf16[1,16,1024]{2,1,0:T(8,128)(2,1)S(1)}, bf16[1,16,1024]{2,1,0:T(8,128)(2,1)S(1)}, u32[]{:S(2)}, u32[]{:S(2)}) collective-permute-start(bf16[1,16,1024]{2,1,0:T(8,128)(2,1)S(1)} %get-tuple-element.52), channel_id=1, source_target_pairs={{4,0},{5,1},{6,2},{7,3},{12,8},{13,9},{14,10},{15,11},{20,16},{21,... | collective-permute-start | bytes 98312 | tf_op jit(solution)/shard_map/ppermute | solution.py:29
  13.3 9.9 %collective-permute-start = (bf16[1,16,1024]{2,1,0:T(8,128)(2,1)S(1)}, bf16[1,16,1024]{2,1,0:T(8,128)(2,1)S(1)}, u32[]{:S(2)}, u32[]{:S(2)}) collective-permute-start(bf16[1,16,1024]{2,1,0:T(8,128)(2,1)S(1)} %get-tuple-element.51), channel_id=1, source_target_pairs={{0,4},{1,5},{2,6},{3,7},{8,12},{9,13},{10,14},{11,15},{16,20},{17,... | collective-permute-start | bytes 98312 | tf_op jit(solution)/shard_map/ppermute | solution.py:27
  19.2 23.1 %all-to-all-start.2 = ((bf16[8,8,4,256]{3,1,2,0:T(8,128)(2,1)}), bf16[8,8,4,256]{3,1,2,0:T(8,128)(2,1)}, u32[]{:S(2)}, u32[]{:S(2)}) async-start(bf16[8,8,4,256]{3,1,2,0:T(8,128)(2,1)} %bitcast.44), calls=%async_computation.2 | async-start | bytes 262144 | tf_op jit(solution)/shard_map/all_to_all | solution.py:135
  23.3 4.5 %collective-permute-start.3 = (bf16[18,1,1024]{2,1,0:T(2,128)(2,1)S(1)}, bf16[18,1,1024]{2,1,0:T(2,128)(2,1)S(1)}, u32[]{:S(2)}, u32[]{:S(2)}) collective-permute-start(bf16[18,1,1024]{2,1,0:T(2,128)(2,1)S(1)} %get-tuple-element.50), channel_id=1, source_target_pairs={{1,0},{2,1},{3,2},{5,4},{6,5},{7,6},{9,8},{10,9},{11,10},{13,12},{... | collective-permute-start | bytes 110600 | tf_op jit(solution)/shard_map/ppermute | solution.py:29
  24.6 3.9 %collective-permute-start.2 = (bf16[18,1,1024]{2,1,0:T(2,128)(2,1)S(1)}, bf16[18,1,1024]{2,1,0:T(2,128)(2,1)S(1)}, u32[]{:S(2)}, u32[]{:S(2)}) collective-permute-start(bf16[18,1,1024]{2,1,0:T(2,128)(2,1)S(1)} %get-tuple-element.49), channel_id=1, source_target_pairs={{0,1},{1,2},{2,3},{4,5},{5,6},{6,7},{8,9},{9,10},{10,11},{12,13},{... | collective-permute-start | bytes 110600 | tf_op jit(solution)/shard_map/ppermute | solution.py:27
  27.7 1.5 copy-start.30
  27.7 1.5 copy-start.32
  27.7 1.5 copy-start.34
  27.7 1.5 copy-start.36
  27.8 1.5 copy-start.38
  27.8 1.5 copy-start.40
  27.8 1.5 copy-start.42
  30.4 1.3 copy-start.5
  31.6 4.8 %copy-start.7 = (bf16[2,8,2,8,256]{4,3,1,2,0:T(8,128)(2,1)}, bf16[2,8,2,8,256]{4,3,1,2,0:T(8,128)(2,1)S(1)}, u32[]{:S(2)}) copy-start(bf16[2,8,2,8,256]{4,3,1,2,0:T(8,128)(2,1)S(1)} %copy.133) | copy-start | bytes 393220
  32.2 4.2 %copy-start.18 = (bf16[4,64,256]{1,2,0:T(8,128)(2,1)}, bf16[4,64,256]{1,2,0:T(8,128)(2,1)S(1)}, u32[]{:S(2)}) copy-start(bf16[4,64,256]{1,2,0:T(8,128)(2,1)S(1)} %copy.134) | copy-start | bytes 393220
  33.3 3.2 copy-start.26
  42.3 12.4 %all-to-all-start = ((bf16[8,8,4,256]{3,1,2,0:T(8,128)(2,1)}), bf16[8,8,4,256]{3,1,2,0:T(8,128)(2,1)}, u32[]{:S(2)}, u32[]{:S(2)}) async-start(bf16[8,8,4,256]{3,1,2,0:T(8,128)(2,1)} %bitcast.24), calls=%async_computation | async-start | bytes 262144 | tf_op jit(solution)/shard_map/all_to_all | solution.py:135
  49.1 119.4 %reduce-scatter.16.cloned.1.call-start = ((), (), s32[]{:S(2)}) async-start(), calls=%async_computation.15 | async-start | bytes 327680 | tf_op jit(solution)/shard_map/reduce_scatter | solution.py:284
  57.0 7.6 %copy-start.17 = (bf16[4,64,8,32]{1,3,2,0:T(8,128)(2,1)S(1)}, bf16[4,64,8,32]{1,3,2,0:T(8,128)(2,1)}, u32[]{:S(2)}) copy-start(bf16[4,64,8,32]{1,3,2,0:T(8,128)(2,1)} %copy.154) | copy-start | bytes 393220
  64.7 4.0 %copy-start.49 = (f32[4,8,64]{2,1,0:T(8,128)}, f32[4,8,64]{2,1,0:T(8,128)S(1)}, u32[]{:S(2)}) copy-start(f32[4,8,64]{2,1,0:T(8,128)S(1)} %get-tuple-element.80) | copy-start | bytes 24580
  64.7 1.9 copy-start.16
  64.7 1.9 copy-start.29
  69.8 7.0 %copy-start.4 = (bf16[256,768]{1,0:T(8,128)(2,1)S(1)}, bf16[256,768]{1,0:T(8,128)(2,1)}, u32[]{:S(2)}) copy-start(bf16[256,768]{1,0:T(8,128)(2,1)} %param.22) | copy-start | bytes 1179652
  77.1 12.6 %copy-start.9 = (bf16[1,16,16,256]{3,2,1,0:T(8,128)(2,1)S(1)}, bf16[1,16,16,256]{3,2,1,0:T(8,128)(2,1)}, u32[]{:S(2)}) copy-start(bf16[1,16,16,256]{3,2,1,0:T(8,128)(2,1)} %param.13) | copy-start | bytes 393220
  87.2 4.0 %copy-start.12 = (bf16[2,8,2,8,256]{4,3,2,1,0:T(8,128)(2,1)S(1)}, bf16[2,8,2,8,256]{4,3,2,1,0:T(8,128)(2,1)}, u32[]{:S(2)}) copy-start(bf16[2,8,2,8,256]{4,3,2,1,0:T(8,128)(2,1)} %copy-done.11) | copy-start | bytes 393220
  92.2 76.3 %reduce-scatter.20.cloned.1.call-start = ((), (), s32[]{:S(2)}) async-start(), calls=%async_computation.17 | async-start | bytes 327680 | tf_op jit(solution)/shard_map/reduce_scatter | solution.py:287
  94.7 22.0 %copy-start.3 = (bf16[4,64,768]{2,1,0:T(8,128)(2,1)S(1)}, bf16[4,64,768]{2,1,0:T(8,128)(2,1)}, u32[]{:S(2)}) copy-start(bf16[4,64,768]{2,1,0:T(8,128)(2,1)} %copy-done.2) | copy-start | bytes 1179652
  115.3 53.2 %reduce-scatter.18.cloned.1.call-start = ((), (), s32[]{:S(2)}) async-start(), calls=%async_computation.16 | async-start | bytes 983040 | tf_op jit(solution)/shard_map/reduce_scatter | solution.py:286
  117.9 66.2 %reduce-scatter.14.cloned.1.call-start = ((), (), s32[]{:S(2)}) async-start(), calls=%async_computation.14 | async-start | bytes 983040 | tf_op jit(solution)/shard_map/reduce_scatter | solution.py:283
  122.1 2.0 copy-start.15
  122.1 2.0 copy-start.27
  124.0 1.9 copy-start.24
  124.0 1.9 copy-start.50
  124.0 3.0 copy-start.25
  131.2 5.2 %copy-start.6 = (bf16[256,768]{1,0:T(8,128)(2,1)S(1)}, bf16[256,768]{1,0:T(8,128)(2,1)}, u32[]{:S(2)}) copy-start(bf16[256,768]{1,0:T(8,128)(2,1)} %param.19) | copy-start | bytes 1179652
  136.4 2.6 copy-start.47
  138.9 73.9 %reduce-scatter.12.cloned.1.call-start = ((), (), s32[]{:S(2)}) async-start(), calls=%async_computation.13 | async-start | bytes 1310720 | tf_op jit(solution)/shard_map/reduce_scatter | solution.py:281
  138.9 2.2 copy-start.23
  139.0 3.3 copy-start.14
  142.2 1.8 copy-start.31
  142.2 1.8 copy-start.33
  142.2 1.8 copy-start.35
  142.3 1.8 copy-start.37
  142.3 1.8 copy-start.39
  142.3 1.8 copy-start.41
  142.3 1.8 copy-start.43
  143.9 16.0 %copy-start.48 = (f32[256]{0:T(256)S(1)}, f32[256]{0:T(256)}, u32[]{:S(2)}) copy-start(f32[256]{0:T(256)} %param.14) | copy-start | bytes 3076
  144.0 97.0 %reduce-scatter.8.cloned.1.call-start = ((), (), s32[]{:S(2)}) async-start(), calls=%async_computation.11 | async-start | bytes 1310720 | tf_op jit(solution)/shard_map/reduce_scatter | solution.py:279
  147.8 6.2 %collective-permute-start.5 = (f32[1,16,1024]{2,1,0:T(8,128)S(1)}, f32[1,16,1024]{2,1,0:T(8,128)S(1)}, u32[]{:S(2)}, u32[]{:S(2)}) collective-permute-start(f32[1,16,1024]{2,1,0:T(8,128)S(1)} %get-tuple-element.48), channel_id=1, source_target_pairs={{4,0},{5,1},{6,2},{7,3},{12,8},{13,9},{14,10},{15,11},{20,16},{21,... | collective-permute-start | bytes 196616 | tf_op jit(solution)/shard_map/ppermute | solution.py:29
  149.1 6.4 %collective-permute-start.4 = (f32[1,16,1024]{2,1,0:T(8,128)S(1)}, f32[1,16,1024]{2,1,0:T(8,128)S(1)}, u32[]{:S(2)}, u32[]{:S(2)}) collective-permute-start(f32[1,16,1024]{2,1,0:T(8,128)S(1)} %get-tuple-element.47), channel_id=1, source_target_pairs={{0,4},{1,5},{2,6},{3,7},{8,12},{9,13},{10,14},{11,15},{16,20},{17,... | collective-permute-start | bytes 196616 | tf_op jit(solution)/shard_map/ppermute | solution.py:27
  155.6 4.5 %collective-permute-start.6 = (f32[18,1,1024]{2,1,0:T(1,128)S(1)}, f32[18,1,1024]{2,1,0:T(1,128)S(1)}, u32[]{:S(2)}, u32[]{:S(2)}) collective-permute-start(f32[18,1,1024]{2,1,0:T(1,128)S(1)} %get-tuple-element.45), channel_id=1, source_target_pairs={{1,0},{2,1},{3,2},{5,4},{6,5},{7,6},{9,8},{10,9},{11,10},{13,12},{... | collective-permute-start | bytes 221192 | tf_op jit(solution)/shard_map/ppermute | solution.py:29
  156.9 3.9 %collective-permute-start.7 = (f32[18,1,1024]{2,1,0:T(1,128)S(1)}, f32[18,1,1024]{2,1,0:T(1,128)S(1)}, u32[]{:S(2)}, u32[]{:S(2)}) collective-permute-start(f32[18,1,1024]{2,1,0:T(1,128)S(1)} %get-tuple-element.46), channel_id=1, source_target_pairs={{0,1},{1,2},{2,3},{4,5},{5,6},{6,7},{8,9},{9,10},{10,11},{12,13},{... | collective-permute-start | bytes 221192 | tf_op jit(solution)/shard_map/ppermute | solution.py:27
  163.3 1.5 copy-start.53
  163.3 2.7 copy-start.10
  163.3 3.5 %copy-start.21 = (bf16[256,256]{1,0:T(8,128)(2,1)S(1)}, bf16[256,256]{1,0:T(8,128)(2,1)}, u32[]{:S(2)}) copy-start(bf16[256,256]{1,0:T(8,128)(2,1)} %param.23) | copy-start | bytes 393220
  164.6 96.8 %reduce-scatter.10.cloned.1.call-start = ((), (), s32[]{:S(2)}) async-start(), calls=%async_computation.12 | async-start | bytes 81920 | tf_op jit(solution)/shard_map/reduce_scatter | solution.py:280
  167.6 73.6 %copy-start.51 = (f32[256]{0:T(256)S(1)}, f32[256]{0:T(256)}, u32[]{:S(2)}) copy-start(f32[256]{0:T(256)} %get-tuple-element.21) | copy-start | bytes 3076
  167.6 73.6 %copy-start.52 = (f32[256]{0:T(256)S(1)}, f32[256]{0:T(256)}, u32[]{:S(2)}) copy-start(f32[256]{0:T(256)} %get-tuple-element.23) | copy-start | bytes 3076
  167.6 154.2 %all-reduce.23.cloned.1.call-start = ((), (), s32[]{:S(2)}) async-start(), calls=%async_computation.18 | async-start | bytes 2097152 | tf_op jit(solution)/shard_map/psum | solution.py:262
  321.9 8.1 %copy-start.44 = (f32[64,256]{1,0:T(8,128)S(1)}, f32[64,256]{1,0:T(8,128)}, u32[]{:S(2)}) copy-start(f32[64,256]{1,0:T(8,128)} %get-tuple-element.97) | copy-start | bytes 196612
  (8 other events, 7.8 us)
Sparse Core Ops, SparseCore 0:
  92.4 20.0 reduce-scatter.15
  115.4 20.1 reduce-scatter.19
  137.9 21.5 reduce-scatter.17
  161.6 22.3 reduce-scatter.13
  186.2 26.5 reduce-scatter.11
  215.1 25.7 reduce-scatter.7
  243.7 17.6 reduce-scatter.9
  265.7 56.1 all-reduce.22
where the time goes:
time: 339 us; the launch traced here: 337 us
  waiting for transfers between devices  124 us (37%)
  local copies, waits for them, and re-layouts  51.3 us (15%)
  blocking collectives  48.9 us (14%)
  matrix products  42.2 us (12%)
  starting transfers between devices  32 us (9%)
  other arithmetic  23 us (7%)
  between operations  16 us (5%)
    psum x1, waiting for transfers between devices, body(): lax.psum((local_grads[0], local_grads[1], local_grads[2], local_grads[3],...  35.9 us
    reduce_scatter x1, waiting for transfers between devices, body(): lax.psum_scatter(whole_sums[3], 'rep', scatter_dimension=0, tiled=True)  28.8 us
    reduce_scatter x1, waiting for transfers between devices, body(): lax.psum_scatter(whole_sums[1], 'rep', scatter_dimension=0, tiled=True)  28.1 us
    psum x1, blocking collectives, body(): lax.psum((local_grads[0], local_grads[1], local_grads[2], local_grads[3],...  23.7 us
    all_to_all x2, blocking collectives, swap_blocks(): lax.all_to_all(as_sent(flattened), ('sy', 'sx'), split_axis=0, concat_axi...  15.8 us
    reduce_scatter x1, waiting for transfers between devices, body(): lax.psum_scatter(whole_sums[5], 'rep', scatter_dimension=0, tiled=True)  15.5 us
    ppermute x4, starting transfers between devices, extended_2(): lax.ppermute(tail, axis, [(i, (i + 1) % count) for i in range(ends)])  15.5 us
    unnamed x118, local copies, waits for them, and re-layouts  11.9 us
  transfers between devices with their start and end apart: 18, of which 10 were waited for; matrix products, arithmetic and copies ran while one was open for 21% of the time, Pallas kernels for 0%

commit v1 on v0

--- a/solution.py
+++ b/solution.py
@@ -259,7 +259,7 @@
         outer_sum(grid_windows, tap_grid_in),
         outer_sum(grid_home, tap_grid_out),
     )
-    whole_sums = lax.psum(
+    partial = lax.psum(
         (
             local_grads[0],
             local_grads[1],
@@ -272,8 +272,9 @@
             local_grads[8],
             local_grads[9],
         ),
-        ("sy", "sx"),
-    )
+        "sx",
+    )
+    whole_sums = lax.psum(partial, "sy")
     summed = (
         lax.psum_scatter(whole_sums[0], "rep", scatter_dimension=0, tiled=True),
         lax.psum_scatter(whole_sums[1], "rep", scatter_dimension=0, tiled=True),

time: 339 us -> 361 us (1.065)
  waiting for transfers between devices: 124 us -> 147 us
    psum x0 -> x1, waiting for transfers between devices: none -> 21.5 us  [body(): whole_sums = lax.psum(partial, 'sy')]
    psum x1, blocking collectives: 23.7 us -> 10.6 us  [body(): lax.psum((local_grads[0], local_grads[1], local_grads[2], local_grads[3],...]
    psum x0 -> x1, blocking collectives: none -> 9.37 us  [body(): whole_sums = lax.psum(partial, 'sy')]
    reduce_scatter x1, waiting for transfers between devices: 15.5 us -> 19.5 us  [body(): lax.psum_scatter(whole_sums[5], 'rep', scatter_dimension=0, tiled=True)]
  transfers between devices with their start and end apart: 18 -> 19, of which waited for: 10 -> 11; matrix products, arithmetic and copies ran while one was open for 21% -> 20% of each run, Pallas kernels for 0% -> 0%
where the time goes in v1:
time: 361 us; the launch traced here: 359 us
  waiting for transfers between devices  147 us (41%)
  local copies, waits for them, and re-layouts  51.3 us (14%)
  blocking collectives  47.5 us (13%)
  matrix products  42.2 us (12%)
  starting transfers between devices  32.1 us (9%)
  other arithmetic  23 us (6%)
  between operations  15.7 us (4%)
    psum x1, waiting for transfers between devices, body(): lax.psum((local_grads[0], local_grads[1], local_grads[2], local_grads[3],...  34.8 us
    reduce_scatter x1, waiting for transfers between devices, body(): lax.psum_scatter(whole_sums[3], 'rep', scatter_dimension=0, tiled=True)  28.5 us
    reduce_scatter x1, waiting for transfers between devices, body(): lax.psum_scatter(whole_sums[1], 'rep', scatter_dimension=0, tiled=True)  28.1 us
    psum x1, waiting for transfers between devices, body(): whole_sums = lax.psum(partial, 'sy')  21.5 us
    reduce_scatter x1, waiting for transfers between devices, body(): lax.psum_scatter(whole_sums[5], 'rep', scatter_dimension=0, tiled=True)  19.5 us
    all_to_all x2, blocking collectives, swap_blocks(): lax.all_to_all(as_sent(flattened), ('sy', 'sx'), split_axis=0, concat_axi...  15.8 us
    ppermute x4, starting transfers between devices, extended_2(): lax.ppermute(tail, axis, [(i, (i + 1) % count) for i in range(ends)])  15.5 us
    unnamed x118, local copies, waits for them, and re-layouts  11.9 us
  transfers between devices with their start and end apart: 19, of which 11 were waited for; matrix products, arithmetic and copies ran while one was open for 20% of the time, Pallas kernels for 0%

profile of v1, /device:TPU:0, one launch (start us, length us, event | category | flops | bytes accessed | tf_op | source)
XLA Modules:
  0.0 359.2 jit_solution(12068429778434549525)
XLA Ops:
  9.5 2.4 multiply_convert_fusion.1
  11.8 1.4 collective-permute-start.1
  13.3 4.9 %collective-permute-start = (bf16[1,16,1024]{2,1,0:T(8,128)(2,1)S(1)}, bf16[1,16,1024]{2,1,0:T(8,128)(2,1)S(1)}, u32[]{:S(2)}, u32[]{:S(2)}) collective-permute-start(bf16[1,16,1024]{2,1,0:T(8,128)(2,1)S(1)} %get-tuple-element.61), channel_id=1, source_target_pairs={{0,4},{1,5},{2,6},{3,7},{8,12},{9,13},{10,14},{11,15},{16,20},{17,... | collective-permute-start | bytes 98312 | tf_op jit(solution)/shard_map/ppermute | solution.py:27
  19.2 4.0 %all-to-all-start.2 = ((bf16[8,8,4,256]{3,1,2,0:T(8,128)(2,1)}), bf16[8,8,4,256]{3,1,2,0:T(8,128)(2,1)}, u32[]{:S(2)}, u32[]{:S(2)}) async-start(bf16[8,8,4,256]{3,1,2,0:T(8,128)(2,1)} %bitcast.44), calls=%async_computation.2 | async-start | bytes 262144 | tf_op jit(solution)/shard_map/all_to_all | solution.py:135
  23.3 1.3 collective-permute-start.3
  24.6 3.0 collective-permute-start.2
  33.3 3.2 fusion.105
  36.5 1.5 fusion.6
  42.3 6.8 %all-to-all-start = ((bf16[8,8,4,256]{3,1,2,0:T(8,128)(2,1)}), bf16[8,8,4,256]{3,1,2,0:T(8,128)(2,1)}, u32[]{:S(2)}, u32[]{:S(2)}) async-start(bf16[8,8,4,256]{3,1,2,0:T(8,128)(2,1)} %bitcast.24), calls=%async_computation | async-start | bytes 262144 | tf_op jit(solution)/shard_map/all_to_all | solution.py:135
  50.8 1.2 reshape_reshape.26
  53.1 1.6 all-to-all-done
  55.8 1.3 convolution_convert_fusion.3
  57.8 1.7 copy.143
  59.6 1.7 copy.144
  62.1 2.5 fusion.107
  64.7 1.8 fusion.15
  69.8 1.8 copy.160
  71.6 1.7 copy.158
  73.3 1.7 copy.156
  77.4 7.9 %all_to_all.20 = bf16[8,8,4,256]{3,1,2,0:T(8,128)(2,1)S(1)} all-to-all(bf16[8,8,4,256]{3,1,2,0:T(8,128)(2,1)S(1)} %bitcast.291), channel_id=1, replica_groups=mesh['rep'=4,'sy'=2,'sx'=4] {'sy','sx'}, dimensions={0} | all-to-all | bytes 262144 | tf_op jit(solution)/shard_map/all_to_all | solution.py:135
  88.2 1.5 multiply_reduce_fusion.9
  89.8 1.6 fusion.96
  92.5 2.2 fusion.7
  94.8 2.1 copy.147
  96.8 2.1 reshape.413
  98.9 1.7 copy.148
  100.6 1.6 reshape_reshape.24
  103.2 7.9 %all_to_all.21 = bf16[8,8,4,256]{3,1,2,0:T(8,128)(2,1)S(1)} all-to-all(bf16[8,8,4,256]{3,1,2,0:T(8,128)(2,1)S(1)} %bitcast.293), channel_id=1, replica_groups=mesh['rep'=4,'sy'=2,'sx'=4] {'sy','sx'}, dimensions={0} | all-to-all | bytes 262144 | tf_op jit(solution)/shard_map/all_to_all | solution.py:135
  111.8 1.6 reshape_reshape.29
  113.4 1.9 fusion.112
  115.4 1.3 multiply_divide_fusion
  116.7 1.2 fusion.111
  118.0 1.2 fusion.114
  119.9 1.2 reshape.428
  122.1 1.9 fusion.20
  124.1 1.9 convolution_convert_fusion.5
  127.1 2.5 convolution_convert_fusion.6
  129.6 1.7 copy.170
  131.3 2.4 convolution_convert_fusion.7
  133.7 1.7 copy.167
  136.8 2.1 fusion.109
  142.4 1.6 convolution_bitcast_fusion
  144.2 3.7 %multiply_reduce_fusion.8 = (f32[1024]{0:T(1024)S(1)}, f32[1024]{0:T(1024)S(1)}, f32[1024]{0:T(1024)S(1)}, f32[1024]{0:T(1024)S(1)}, f32[1024]{0:T(1024)S(1)}, /...) fusion(f32[18,18,1024]{2,1,0:T(8,128)S(1)} %convert_element_typ, ...), kind=kLoop, calls=%fused_computation.104 | loop fusion | flops 14408704 | bytes 11083776 | tf_op jit(solution)/shard_map/transpose(jvp())/reduce_sum | solution.py:112
  147.8 1.3 collective-permute-start.5
  149.1 4.5 %collective-permute-start.4 = (f32[1,16,1024]{2,1,0:T(8,128)S(1)}, f32[1,16,1024]{2,1,0:T(8,128)S(1)}, u32[]{:S(2)}, u32[]{:S(2)}) collective-permute-start(f32[1,16,1024]{2,1,0:T(8,128)S(1)} %get-tuple-element.57), channel_id=1, source_target_pairs={{0,4},{1,5},{2,6},{3,7},{8,12},{9,13},{10,14},{11,15},{16,20},{17,... | collective-permute-start | bytes 196616 | tf_op jit(solution)/shard_map/ppermute | solution.py:27
  154.0 1.6 collective-permute-done.4
  155.7 1.3 collective-permute-start.6
  157.0 3.0 collective-permute-start.7
  161.4 1.9 fusion.22
  163.4 1.3 fusion.108
  164.9 19.5 %reduce-scatter.14.cloned.1.call-done = f32[64,768]{1,0:T(8,128)} async-done(((f32[256,768]{1,0:T(8,128)}), f32[64,768]{1,0:T(8,128)}) %reduce-scatter.14.cloned.1.call-update) | async-done | bytes 196624 | tf_op jit(solution)/shard_map/reduce_scatter | solution.py:284
  184.4 28.5 %reduce-scatter.12.cloned.1.call-done = f32[256,256]{1,0:T(8,128)} async-done(((f32[1024,256]{1,0:T(8,128)}), f32[256,256]{1,0:T(8,128)}) %reduce-scatter.12.cloned.1.call-update) | async-done | bytes 262160 | tf_op jit(solution)/shard_map/reduce_scatter | solution.py:282
  212.9 28.1 %reduce-scatter.8.cloned.1.call-done = f32[64,1024]{1,0:T(8,128)} async-done(((f32[256,1024]{1,0:T(8,128)}), f32[64,1024]{1,0:T(8,128)}) %reduce-scatter.8.cloned.1.call-update) | async-done | bytes 262160 | tf_op jit(solution)/shard_map/reduce_scatter | solution.py:280
  244.7 34.8 %all-reduce.26.cloned.1.call-done = (f32[64,1024]{1,0:T(8,128)}, f32[256,256]{1,0:T(8,128)}, f32[64,768]{1,0:T(8,128)}, f32[64,256]{1,0:T(8,128)}, f32[64,768]{1,0:T(8,128)}, /*index=5*/f32[64,256]{1,0:T(8,128)}) async-done(((f32[64,1024]{1,0:T(8,128)}, f32[256,256]{1,0:T(8,128)}, f32[64,768]{1,0:T(8,128)}, f32[64,256]{1,0:T(8,128)}, f32[64,768]{1,0:T(8,128)}, /*index=5*/f32[64,256]{1,0:T(8,128)}), ...) | async-done | bytes 1048592 | tf_op jit(solution)/shard_map/psum | solution.py:262
  280.0 11.7 %all-reduce.20 = (f32[256]{0:T(256)S(1)}, f32[256]{0:T(256)S(1)}, f32[256]{0:T(256)S(1)}) all-reduce(f32[256]{0:T(256)S(1)} %get-tuple-element.25, f32[256]{0:T(256)S(1)} %copy-done.52, f32[256]{0:T(256)S(1)} %copy-done.51), channel_id=2, replica_groups=mesh['rep'=4,'sy'=2,'sx'=4] {'rep'}, use_global_device_ids=true, to_apply=%region_21.0.clone | all-reduce | flops 768 | bytes 6144
  291.9 9.7 %reduce-scatter.10.cloned.1.call-done = f32[256,9]{0,1:T(8,128)} async-done(((f32[1024,9]{0,1:T(8,128)}), f32[256,9]{0,1:T(8,128)}) %reduce-scatter.10.cloned.1.call-update) | async-done | bytes 9232 | tf_op jit(solution)/shard_map/reduce_scatter | solution.py:281
  301.6 10.6 %all-reduce.18 = (f32[64]{0:T(128)S(1)}, f32[256,9]{0,1:T(8,128)S(1)}, f32[64]{0:T(128)S(1)}, f32[64]{0:T(128)S(1)}) all-reduce(f32[64]{0:T(128)S(1)} %dynamic-slice.1, f32[256,9]{0,1:T(8,128)} %reduce-scatter.10.cloned.1.call-done, f32[64]{0:T(128)S(1)} %dynamic-slice.3, ...), channel_id=1, replica_groups=mesh['rep'=4,'sy'=2,'sx'=4] {'sx'}, use_global_device_ids=true, to_apply=%region_19.0 | all-reduce | flops 2496 | bytes 19968 | tf_op jit(solution)/shard_map/psum | solution.py:262
  312.2 9.4 %all-reduce.21 = (f32[64]{0:T(128)}, f32[256,9]{0,1:T(8,128)}, f32[64]{0:T(128)}, f32[64]{0:T(128)}) all-reduce(f32[64]{0:T(128)S(1)} %get-tuple-element.27, f32[256,9]{0,1:T(8,128)S(1)} %get-tuple-element.28, f32[64]{0:T(128)S(1)} %get-tuple-element.29, f32[64]{0:T(128)S(1)} %get-tuple-element.30), channel_id=1, replica_groups=mesh['rep'=4,'sy'=2,'sx'=4] {'sy'}, use_global_device_ids=true, to_apply=%region_20.0 | all-reduce | flops 2496 | bytes 19968 | tf_op jit(solution)/shard_map/psum | solution.py:277
  322.5 21.5 %all-reduce.28.cloned.1.call-done = (f32[64,1024]{1,0:T(8,128)}, f32[256,256]{1,0:T(8,128)}, f32[64,768]{1,0:T(8,128)}, f32[64,256]{1,0:T(8,128)}, f32[64,768]{1,0:T(8,128)}, /*index=5*/f32[64,256]{1,0:T(8,128)}) async-done(((f32[64,1024]{1,0:T(8,128)}, f32[256,256]{1,0:T(8,128)}, f32[64,768]{1,0:T(8,128)}, f32[64,256]{1,0:T(8,128)}, f32[64,768]{1,0:T(8,128)}, /*index=5*/f32[64,256]{1,0:T(8,128)}), ...) | async-done | bytes 1048592 | tf_op jit(solution)/shard_map/psum | solution.py:277
  344.0 1.7 copy.205
  345.7 1.7 copy.206
  347.3 1.6 copy.207
  349.0 1.5 copy.208
  350.4 1.6 copy.209
  (235 shorter events, 44.5 us)
Async XLA Ops:
  7.2 2.3 copy-start
  8.3 9.9 %copy-start.8 = (bf16[1,16,16,256]{3,2,1,0:T(8,128)(2,1)S(1)}, bf16[1,16,16,256]{3,2,1,0:T(8,128)(2,1)}, u32[]{:S(2)}) copy-start(bf16[1,16,16,256]{3,2,1,0:T(8,128)(2,1)} %param.13) | copy-start | bytes 393220
  8.3 9.9 %copy-start.20 = (bf16[256,256]{1,0:T(8,128)(2,1)S(1)}, bf16[256,256]{1,0:T(8,128)(2,1)}, u32[]{:S(2)}) copy-start(bf16[256,256]{1,0:T(8,128)(2,1)} %param.23) | copy-start | bytes 393220
  11.8 15.9 %copy-start.45 = (f32[1024,9]{0,1:T(8,128)S(1)}, f32[1024,9]{0,1:T(8,128)}, u32[]{:S(2)}) copy-start(f32[1024,9]{0,1:T(8,128)} %param.16) | copy-start | bytes 110596
  11.8 11.4 %collective-permute-start.1 = (bf16[1,16,1024]{2,1,0:T(8,128)(2,1)S(1)}, bf16[1,16,1024]{2,1,0:T(8,128)(2,1)S(1)}, u32[]{:S(2)}, u32[]{:S(2)}) collective-permute-start(bf16[1,16,1024]{2,1,0:T(8,128)(2,1)S(1)} %get-tuple-element.62), channel_id=1, source_target_pairs={{4,0},{5,1},{6,2},{7,3},{12,8},{13,9},{14,10},{15,11},{20,16},{21,... | collective-permute-start | bytes 98312 | tf_op jit(solution)/shard_map/ppermute | solution.py:29
  13.3 9.9 %collective-permute-start = (bf16[1,16,1024]{2,1,0:T(8,128)(2,1)S(1)}, bf16[1,16,1024]{2,1,0:T(8,128)(2,1)S(1)}, u32[]{:S(2)}, u32[]{:S(2)}) collective-permute-start(bf16[1,16,1024]{2,1,0:T(8,128)(2,1)S(1)} %get-tuple-element.61), channel_id=1, source_target_pairs={{0,4},{1,5},{2,6},{3,7},{8,12},{9,13},{10,14},{11,15},{16,20},{17,... | collective-permute-start | bytes 98312 | tf_op jit(solution)/shard_map/ppermute | solution.py:27
  19.2 23.2 %all-to-all-start.2 = ((bf16[8,8,4,256]{3,1,2,0:T(8,128)(2,1)}), bf16[8,8,4,256]{3,1,2,0:T(8,128)(2,1)}, u32[]{:S(2)}, u32[]{:S(2)}) async-start(bf16[8,8,4,256]{3,1,2,0:T(8,128)(2,1)} %bitcast.44), calls=%async_computation.2 | async-start | bytes 262144 | tf_op jit(solution)/shard_map/all_to_all | solution.py:135
  23.3 4.5 %collective-permute-start.3 = (bf16[18,1,1024]{2,1,0:T(2,128)(2,1)S(1)}, bf16[18,1,1024]{2,1,0:T(2,128)(2,1)S(1)}, u32[]{:S(2)}, u32[]{:S(2)}) collective-permute-start(bf16[18,1,1024]{2,1,0:T(2,128)(2,1)S(1)} %get-tuple-element.60), channel_id=1, source_target_pairs={{1,0},{2,1},{3,2},{5,4},{6,5},{7,6},{9,8},{10,9},{11,10},{13,12},{... | collective-permute-start | bytes 110600 | tf_op jit(solution)/shard_map/ppermute | solution.py:29
  24.6 3.9 %collective-permute-start.2 = (bf16[18,1,1024]{2,1,0:T(2,128)(2,1)S(1)}, bf16[18,1,1024]{2,1,0:T(2,128)(2,1)S(1)}, u32[]{:S(2)}, u32[]{:S(2)}) collective-permute-start(bf16[18,1,1024]{2,1,0:T(2,128)(2,1)S(1)} %get-tuple-element.59), channel_id=1, source_target_pairs={{0,1},{1,2},{2,3},{4,5},{5,6},{6,7},{8,9},{9,10},{10,11},{12,13},{... | collective-permute-start | bytes 110600 | tf_op jit(solution)/shard_map/ppermute | solution.py:27
  27.7 1.5 copy-start.30
  27.7 1.5 copy-start.32
  27.7 1.5 copy-start.34
  27.8 1.5 copy-start.36
  27.8 1.5 copy-start.38
  27.8 1.5 copy-start.40
  27.8 1.5 copy-start.42
  31.6 4.8 %copy-start.7 = (bf16[2,8,2,8,256]{4,3,1,2,0:T(8,128)(2,1)}, bf16[2,8,2,8,256]{4,3,1,2,0:T(8,128)(2,1)S(1)}, u32[]{:S(2)}) copy-start(bf16[2,8,2,8,256]{4,3,1,2,0:T(8,128)(2,1)S(1)} %copy.133) | copy-start | bytes 393220
  32.3 4.2 %copy-start.18 = (bf16[4,64,256]{1,2,0:T(8,128)(2,1)}, bf16[4,64,256]{1,2,0:T(8,128)(2,1)S(1)}, u32[]{:S(2)}) copy-start(bf16[4,64,256]{1,2,0:T(8,128)(2,1)S(1)} %copy.134) | copy-start | bytes 393220
  33.3 3.2 copy-start.26
  42.3 12.4 %all-to-all-start = ((bf16[8,8,4,256]{3,1,2,0:T(8,128)(2,1)}), bf16[8,8,4,256]{3,1,2,0:T(8,128)(2,1)}, u32[]{:S(2)}, u32[]{:S(2)}) async-start(bf16[8,8,4,256]{3,1,2,0:T(8,128)(2,1)} %bitcast.24), calls=%async_computation | async-start | bytes 262144 | tf_op jit(solution)/shard_map/all_to_all | solution.py:135
  49.1 115.7 %reduce-scatter.16.cloned.1.call-start = ((), (), s32[]{:S(2)}) async-start(), calls=%async_computation.15 | async-start | bytes 327680 | tf_op jit(solution)/shard_map/reduce_scatter | solution.py:285
  57.1 7.6 %copy-start.17 = (bf16[4,64,8,32]{1,3,2,0:T(8,128)(2,1)S(1)}, bf16[4,64,8,32]{1,3,2,0:T(8,128)(2,1)}, u32[]{:S(2)}) copy-start(bf16[4,64,8,32]{1,3,2,0:T(8,128)(2,1)} %copy.154) | copy-start | bytes 393220
  64.7 4.1 %copy-start.49 = (f32[4,8,64]{2,1,0:T(8,128)}, f32[4,8,64]{2,1,0:T(8,128)S(1)}, u32[]{:S(2)}) copy-start(f32[4,8,64]{2,1,0:T(8,128)S(1)} %get-tuple-element.90) | copy-start | bytes 24580
  64.7 1.9 copy-start.16
  64.7 1.9 copy-start.29
  69.8 7.1 %copy-start.4 = (bf16[256,768]{1,0:T(8,128)(2,1)S(1)}, bf16[256,768]{1,0:T(8,128)(2,1)}, u32[]{:S(2)}) copy-start(bf16[256,768]{1,0:T(8,128)(2,1)} %param.22) | copy-start | bytes 1179652
  77.2 12.6 %copy-start.9 = (bf16[1,16,16,256]{3,2,1,0:T(8,128)(2,1)S(1)}, bf16[1,16,16,256]{3,2,1,0:T(8,128)(2,1)}, u32[]{:S(2)}) copy-start(bf16[1,16,16,256]{3,2,1,0:T(8,128)(2,1)} %param.13) | copy-start | bytes 393220
  87.3 4.1 %copy-start.12 = (bf16[2,8,2,8,256]{4,3,2,1,0:T(8,128)(2,1)S(1)}, bf16[2,8,2,8,256]{4,3,2,1,0:T(8,128)(2,1)}, u32[]{:S(2)}) copy-start(bf16[2,8,2,8,256]{4,3,2,1,0:T(8,128)(2,1)} %copy-done.11) | copy-start | bytes 393220
  92.3 72.5 %reduce-scatter.20.cloned.1.call-start = ((), (), s32[]{:S(2)}) async-start(), calls=%async_computation.17 | async-start | bytes 327680 | tf_op jit(solution)/shard_map/reduce_scatter | solution.py:288
  94.8 22.0 %copy-start.3 = (bf16[4,64,768]{2,1,0:T(8,128)(2,1)S(1)}, bf16[4,64,768]{2,1,0:T(8,128)(2,1)}, u32[]{:S(2)}) copy-start(bf16[4,64,768]{2,1,0:T(8,128)(2,1)} %copy-done.2) | copy-start | bytes 1179652
  115.4 49.5 %reduce-scatter.18.cloned.1.call-start = ((), (), s32[]{:S(2)}) async-start(), calls=%async_computation.16 | async-start | bytes 983040 | tf_op jit(solution)/shard_map/reduce_scatter | solution.py:287
  118.0 66.4 %reduce-scatter.14.cloned.1.call-start = ((), (), s32[]{:S(2)}) async-start(), calls=%async_computation.14 | async-start | bytes 983040 | tf_op jit(solution)/shard_map/reduce_scatter | solution.py:284
  122.1 2.0 copy-start.15
  122.1 2.0 copy-start.27
  124.0 1.9 copy-start.24
  124.1 1.9 copy-start.50
  124.1 3.0 copy-start.25
  131.3 5.2 %copy-start.6 = (bf16[256,768]{1,0:T(8,128)(2,1)S(1)}, bf16[256,768]{1,0:T(8,128)(2,1)}, u32[]{:S(2)}) copy-start(bf16[256,768]{1,0:T(8,128)(2,1)} %param.19) | copy-start | bytes 1179652
  136.5 2.5 copy-start.47
  138.9 73.9 %reduce-scatter.12.cloned.1.call-start = ((), (), s32[]{:S(2)}) async-start(), calls=%async_computation.13 | async-start | bytes 1310720 | tf_op jit(solution)/shard_map/reduce_scatter | solution.py:282
  139.0 2.2 copy-start.23
  139.0 3.3 copy-start.14
  142.3 1.8 copy-start.31
  142.3 1.8 copy-start.33
  142.3 1.8 copy-start.35
  142.3 1.8 copy-start.37
  142.4 1.8 copy-start.39
  142.4 1.8 copy-start.41
  142.4 1.8 copy-start.43
  144.0 16.0 %copy-start.48 = (f32[256]{0:T(256)S(1)}, f32[256]{0:T(256)}, u32[]{:S(2)}) copy-start(f32[256]{0:T(256)} %param.14) | copy-start | bytes 3076
  144.0 96.9 %reduce-scatter.8.cloned.1.call-start = ((), (), s32[]{:S(2)}) async-start(), calls=%async_computation.11 | async-start | bytes 1310720 | tf_op jit(solution)/shard_map/reduce_scatter | solution.py:280
  147.8 6.2 %collective-permute-start.5 = (f32[1,16,1024]{2,1,0:T(8,128)S(1)}, f32[1,16,1024]{2,1,0:T(8,128)S(1)}, u32[]{:S(2)}, u32[]{:S(2)}) collective-permute-start(f32[1,16,1024]{2,1,0:T(8,128)S(1)} %get-tuple-element.58), channel_id=1, source_target_pairs={{4,0},{5,1},{6,2},{7,3},{12,8},{13,9},{14,10},{15,11},{20,16},{21,... | collective-permute-start | bytes 196616 | tf_op jit(solution)/shard_map/ppermute | solution.py:29
  149.1 6.4 %collective-permute-start.4 = (f32[1,16,1024]{2,1,0:T(8,128)S(1)}, f32[1,16,1024]{2,1,0:T(8,128)S(1)}, u32[]{:S(2)}, u32[]{:S(2)}) collective-permute-start(f32[1,16,1024]{2,1,0:T(8,128)S(1)} %get-tuple-element.57), channel_id=1, source_target_pairs={{0,4},{1,5},{2,6},{3,7},{8,12},{9,13},{10,14},{11,15},{16,20},{17,... | collective-permute-start | bytes 196616 | tf_op jit(solution)/shard_map/ppermute | solution.py:27
  155.7 4.5 %collective-permute-start.6 = (f32[18,1,1024]{2,1,0:T(1,128)S(1)}, f32[18,1,1024]{2,1,0:T(1,128)S(1)}, u32[]{:S(2)}, u32[]{:S(2)}) collective-permute-start(f32[18,1,1024]{2,1,0:T(1,128)S(1)} %get-tuple-element.55), channel_id=1, source_target_pairs={{1,0},{2,1},{3,2},{5,4},{6,5},{7,6},{9,8},{10,9},{11,10},{13,12},{... | collective-permute-start | bytes 221192 | tf_op jit(solution)/shard_map/ppermute | solution.py:29
  157.0 3.9 %collective-permute-start.7 = (f32[18,1,1024]{2,1,0:T(1,128)S(1)}, f32[18,1,1024]{2,1,0:T(1,128)S(1)}, u32[]{:S(2)}, u32[]{:S(2)}) collective-permute-start(f32[18,1,1024]{2,1,0:T(1,128)S(1)} %get-tuple-element.56), channel_id=1, source_target_pairs={{0,1},{1,2},{2,3},{4,5},{5,6},{6,7},{8,9},{9,10},{10,11},{12,13},{... | collective-permute-start | bytes 221192 | tf_op jit(solution)/shard_map/ppermute | solution.py:27
  163.4 77.7 %copy-start.53 = (u32[32]{0:T(128)S(1)}, u32[32]{0:T(128)}, u32[]{:S(2)}) copy-start(u32[32]{0:T(128)} %constant.75) | copy-start | bytes 388
  163.4 79.0 %copy-start.10 = (bf16[8,2,4,4,256]{4,3,2,1,0:T(4,128)(2,1)S(1)}, bf16[8,2,4,4,256]{4,3,2,1,0:T(4,128)(2,1)}, u32[]{:S(2)}) copy-start(bf16[8,2,4,4,256]{4,3,2,1,0:T(4,128)(2,1)} %copy.150) | copy-start | bytes 393220
  163.4 79.7 %copy-start.21 = (bf16[256,256]{1,0:T(8,128)(2,1)S(1)}, bf16[256,256]{1,0:T(8,128)(2,1)}, u32[]{:S(2)}) copy-start(bf16[256,256]{1,0:T(8,128)(2,1)} %param.23) | copy-start | bytes 393220
  164.7 114.8 %all-reduce.26.cloned.1.call-start = ((), (), s32[]{:S(2)}) async-start(), calls=%async_computation.18 | async-start | bytes 2097152 | tf_op jit(solution)/shard_map/psum | solution.py:262
  241.0 60.6 %reduce-scatter.10.cloned.1.call-start = ((), (), s32[]{:S(2)}) async-start(), calls=%async_computation.12 | async-start | bytes 81920 | tf_op jit(solution)/shard_map/reduce_scatter | solution.py:281
  244.0 100.0 %all-reduce.28.cloned.1.call-start = ((), (), s32[]{:S(2)}) async-start(), calls=%async_computation.19 | async-start | bytes 2097152 | tf_op jit(solution)/shard_map/psum | solution.py:277
  244.0 36.0 %copy-start.51 = (f32[256]{0:T(256)S(1)}, f32[256]{0:T(256)}, u32[]{:S(2)}) copy-start(f32[256]{0:T(256)} %get-tuple-element.21) | copy-start | bytes 3076
  244.0 36.0 %copy-start.52 = (f32[256]{0:T(256)S(1)}, f32[256]{0:T(256)}, u32[]{:S(2)}) copy-start(f32[256]{0:T(256)} %get-tuple-element.23) | copy-start | bytes 3076
  344.0 8.1 %copy-start.44 = (f32[64,256]{1,0:T(8,128)S(1)}, f32[64,256]{1,0:T(8,128)}, u32[]{:S(2)}) copy-start(f32[64,256]{1,0:T(8,128)} %get-tuple-element.107) | copy-start | bytes 196612
  (9 other events, 9.1 us)
Sparse Core Ops, SparseCore 0:
  92.4 20.1 reduce-scatter.15
  115.5 20.1 reduce-scatter.19
  138.0 21.5 reduce-scatter.17
  161.8 22.5 reduce-scatter.13
  186.5 26.3 reduce-scatter.11
  215.1 25.7 reduce-scatter.7
  243.7 35.7 all-reduce.25
  282.4 19.1 reduce-scatter.9
  304.2 39.7 all-reduce.27
